TPU v7x, 128 devices: a whole 4x4x4 slice. The times are simulated.
128 devices in a mesh: rep: 4 (over x), shard: 32 (over z, y, core).
Axes of the slice: x: 4, y: 4, z: 4, core: 2. Of those that a mesh axis runs over, the one named last changes fastest.
Arguments:
- features: bfloat16 [65536, 1024], P(('rep', 'shard')), may hold values from -6 to 6
- cotangent: bfloat16 [65536, 1024], P(('rep', 'shard')), may hold values from -6 to 6
- cross_weight: bfloat16 [1024, 1024], replicated, may hold values from -0.1875 to 0.1875
- cross_bias: float32 [1024], replicated, may hold values from -3 to 3
- emb_table: float32 [131072, 128], P('shard'), may hold values from -6 to 6
- row_accum: float32 [131072], P('shard'), may hold values from 0.5 to 50
- send_bags: int32 [128, 32, 256], P(('rep', 'shard')), may hold values from 0 to 3583, as said below
- slot_counts: int32 [128, 32], P(('rep', 'shard')), may hold values from 64 to 256, as said below
- recv_rows: int32 [128, 32, 256], P(('rep', 'shard')), may hold values from 0 to 4095, as said below
- touched_rows: int32 [32, 2048], P('shard'), may hold values from 0 to 4095, as said below
Outputs:
- weight_grad: float32 [1024, 1024], replicated
- bias_grad: float32 [1024], replicated
- dense_grad: bfloat16 [65536, 128], P(('rep', 'shard'))
- new_table: float32 [131072, 128], P('shard')
- new_accum: float32 [131072], P('shard')
Inputs may be any that keep to these rules, and one draw needn't show every extreme that they name: `send_bags`: bag b * 7 + f of a device is feature f of its sample b. The first slot_counts[d, s] slots of a block are live; in each replica group some shard receives 256 live slots from every device of the group. `recv_rows`: every slot, live or not, names a row listed in touched_rows for the owner's shard. `touched_rows`: ascending and distinct.
All inputs are finite; a program needn't handle non-finite values.
Results may differ from a plain program's by a relative error of at most 0.0055.
Values may be sent and summed in bfloat16 or wider, within the bound.
No kernel may reach another device: no remote copies, remote signals or barrier semaphores. Data moves between devices by JAX's collectives and lax.ppermute only.
A program may use at most 128 MiB of HBM per device.

v0:
```python
import math
import jax
import jax.numpy as jnp
from jax import lax
from jax.sharding import PartitionSpec as P

learn_rate = 0.5
keep_rate = 0.9


def adagrad_rows(table_rows, accum_rows, grads):
    new_accum = accum_rows + jnp.mean(grads * grads, axis=1)
    new_rows = keep_rate * table_rows - learn_rate * grads / jnp.sqrt(new_accum)[:, None]
    return (new_rows, new_accum)


def blocked(count, fn):
    step_rows = math.gcd(count, 512)
    index_blocks = jnp.arange(count, dtype=jnp.int32).reshape(-1, step_rows)
    result = lax.map(fn, index_blocks)
    return result.reshape((count,) + result.shape[2:])


def per_device(
    features,
    cotangent,
    cross_weight,
    cross_bias,
    emb_table,
    row_accum,
    send_bags,
    slot_counts,
    recv_rows,
    touched_rows,
):
    width = emb_table.shape[1]
    shard_rows = emb_table.shape[0]
    total_tokens = features.shape[0] * lax.axis_size("rep") * lax.axis_size("shard")
    scale = 1.0 / jnp.sqrt(jnp.float32(total_tokens))
    linear = jnp.dot(features, cross_weight, preferred_element_type=jnp.float32) + cross_bias
    cot_f = cotangent.astype(jnp.float32)
    gated = (cot_f * features.astype(jnp.float32)).astype(jnp.bfloat16)
    weight_part = lax.dot_general(
        features, gated, (((0,), (0,)), ((), ())), preferred_element_type=jnp.float32
    )
    bias_part = jnp.sum(gated.astype(jnp.float32), axis=0)
    backprop = lax.dot_general(
        gated, cross_weight, (((1,), (1,)), ((), ())), preferred_element_type=jnp.float32
    )
    input_grad = cot_f * linear + backprop + cot_f
    dense_grad = input_grad[:, :width].astype(jnp.bfloat16)
    pooled = input_grad[:, width:].astype(jnp.bfloat16).reshape(-1, width)
    bag_ids = send_bags[0]
    shard_count = bag_ids.shape[0]
    slot_total = bag_ids.shape[1]
    live_mask = jnp.arange(slot_total, dtype=jnp.int32)[None, :] < slot_counts[0][:, None]
    flat_bags = jnp.where(live_mask, bag_ids, -1).reshape(-1)
    bag_range = jnp.arange(pooled.shape[0], dtype=jnp.int32)

    def pick_bags(positions):
        select = (flat_bags[positions][:, None] == bag_range[None, :]).astype(jnp.bfloat16)
        return jnp.dot(select, pooled, preferred_element_type=jnp.float32).astype(jnp.bfloat16)

    outgoing = blocked(shard_count * slot_total, pick_bags).reshape(shard_count, slot_total, width)
    incoming = lax.all_to_all(outgoing, "shard", split_axis=0, concat_axis=0, tiled=True)
    weight_sum, bias_sum = lax.psum((weight_part, bias_part), ("rep", "shard"))
    weight_grad = weight_sum * scale
    bias_grad = bias_sum * scale
    incoming_rows = incoming.reshape(-1, width)
    slot_rows = recv_rows[0].reshape(-1)
    touched = touched_rows[0]
    row_range = jnp.arange(shard_rows, dtype=jnp.int32)
    marks = jnp.any(row_range[:, None] == touched[None, :], axis=1)

    def row_block(row_ids):
        select = (row_ids[:, None] == slot_rows[None, :]).astype(jnp.bfloat16)
        return jnp.dot(select, incoming_rows, preferred_element_type=jnp.float32)

    local_sums = blocked(shard_rows, row_block)
    row_grads = lax.psum(local_sums.astype(jnp.bfloat16), "rep").astype(jnp.float32)
    upd_table, upd_accum = adagrad_rows(emb_table, row_accum, row_grads)
    new_table = jnp.where(marks[:, None], upd_table, emb_table)
    new_accum = jnp.where(marks, upd_accum, row_accum)
    return (weight_grad, bias_grad, dense_grad, new_table, new_accum)


def solution(mesh):
    in_specs = (
        P(("rep", "shard"), None),
        P(("rep", "shard"), None),
        P(),
        P(),
        P("shard", None),
        P("shard"),
        P(("rep", "shard"), None, None),
        P(("rep", "shard"), None),
        P(("rep", "shard"), None, None),
        P("shard", None),
    )
    out_specs = (P(), P(), P(("rep", "shard"), None), P("shard", None), P("shard"))
    return jax.shard_map(
        per_device, mesh=mesh, in_specs=in_specs, out_specs=out_specs, check_vma=False
    )
```

profile of v0, /device:TPU:0, one launch (start us, length us, event | category | flops | bytes accessed | tf_op | source)
XLA Modules:
  0.0 358.1 jit_solution(6436038658471441879)
XLA Ops:
  17.8 102.1 %while.22 = (s32[]{:T(128)}, bf16[16,512,128]{2,1,0:T(8,128)(2,1)}, s32[16,512]{1,0:T(8,128)S(1)}, s32[8192]{0:T(1024)S(1)}, bf16[3584,128]{1,0:T(8,128)(2,1)}, /*index=5*/s32[]{:T(128)}) while((s32[]{:T(128)}, bf16[16,512,128]{2,1,0:T(8,128)(2,1)}, s32[16,512]{1,0:T(8,128)S(1)}, s32[8192]{0:T(1024)S(1)}, ...), condition=%wide.region_5.6_spmd.clone, body=%wide.region_4.5_spmd.clone.sunk | while | flops 471665152 | bytes 1067093 | solution.py:20
  21.0 3.2 fusion.45
  27.4 3.2 fusion.45
  33.8 3.2 fusion.45
  40.1 3.2 fusion.45
  59.3 3.2 fusion.45
  120.0 8.6 %all-to-all-start = ((bf16[32,256,128]{2,1,0:T(8,128)(2,1)}), bf16[32,256,128]{2,1,0:T(8,128)(2,1)}, u32[]{:S(2)}, u32[]{:S(2)}) async-start(bf16[32,256,128]{2,1,0:T(8,128)(2,1)} %bitcast.47), calls=%async_computation | async-start | bytes 4194304 | tf_op jit(solution)/shard_map/all_to_all | solution.py:65
  128.6 4.5 %convolution_bitcast_fusion = f32[1024,1024]{0,1:T(8,128)} fusion(bf16[512,1024]{1,0:T(8,128)(2,1)S(1)} %copy-done.1, bf16[512,1024]{1,0:T(8,128)(2,1)} %param.15), kind=kOutput, calls=%fused_computation.24 | convolution fusion | flops 1075838976 | bytes 6291456 | tf_op jit(solution)/shard_map/dot_general | solution.py:43
  134.8 79.4 %psum.22 = f32[1024]{0:T(1024)S(1)} all-reduce(f32[1024]{0:T(1024)S(1)} %convert_reduce_fusion), channel_id=1, replica_groups=mesh['rep'=4,'shard'=32] {'rep','shard'}, use_global_device_ids=true, to_apply=%region_2.3 | all-reduce | flops 1024 | bytes 8192 | tf_op jit(solution)/shard_map/psum | solution.py:66
  214.2 37.5 %while.21 = (s32[]{:T(128)}, bf16[8,512,128]{2,1,0:T(8,128)(2,1)}, s32[8,512]{1,0:T(8,128)S(1)}, s32[1,32,256]{2,1,0:T(8,128)S(1)}, bf16[8192,128]{1,0:T(8,128)(2,1)}, /*index=5*/s32[]{:T(128)}) while((s32[]{:T(128)}, bf16[8,512,128]{2,1,0:T(8,128)(2,1)}, s32[8,512]{1,0:T(8,128)S(1)}, s32[1,32,256]{2,1,0:T(8,128)S(1)}, ...), condition=%wide.region_7.8_spmd, body=%wide.region_6.7_spmd.sunk | while | flops 1077936128 | bytes 2463829 | solution.py:20
  214.3 4.6 %fusion.43 = bf16[8,512,128]{2,1,0:T(8,128)(2,1)} fusion(bf16[8,512,128]{2,1,0:T(8,128)(2,1)} %get-tuple-element.202, s32[]{:T(128)S(6)} %copy.33, bf16[8192,128]{1,0:T(8,128)(2,1)} %get-tuple-element.211, s32[8192]{0:T(1024)S(1)} %bitcast.50, s32[512]{0:T(512)S(1)} %bitcast.53), kind=kOutput, calls=%fused_computation.7.clone.1 | convolution fusion | flops 1077936128 | bytes 2394116 | tf_op jit(solution)/shard_map/while/body/eval_jaxpr/dot_general | solution.py:77
  219.0 4.6 %fusion.43 = bf16[8,512,128]{2,1,0:T(8,128)(2,1)} fusion(bf16[8,512,128]{2,1,0:T(8,128)(2,1)} %get-tuple-element.202, s32[]{:T(128)S(6)} %copy.33, bf16[8192,128]{1,0:T(8,128)(2,1)} %get-tuple-element.211, s32[8192]{0:T(1024)S(1)} %bitcast.50, s32[512]{0:T(512)S(1)} %bitcast.53), kind=kOutput, calls=%fused_computation.7.clone.1 | convolution fusion | flops 1077936128 | bytes 2394116 | tf_op jit(solution)/shard_map/while/body/eval_jaxpr/dot_general | solution.py:77
  223.6 4.6 %fusion.43 = bf16[8,512,128]{2,1,0:T(8,128)(2,1)} fusion(bf16[8,512,128]{2,1,0:T(8,128)(2,1)} %get-tuple-element.202, s32[]{:T(128)S(6)} %copy.33, bf16[8192,128]{1,0:T(8,128)(2,1)} %get-tuple-element.211, s32[8192]{0:T(1024)S(1)} %bitcast.50, s32[512]{0:T(512)S(1)} %bitcast.53), kind=kOutput, calls=%fused_computation.7.clone.1 | convolution fusion | flops 1077936128 | bytes 2394116 | tf_op jit(solution)/shard_map/while/body/eval_jaxpr/dot_general | solution.py:77
  228.3 4.6 %fusion.43 = bf16[8,512,128]{2,1,0:T(8,128)(2,1)} fusion(bf16[8,512,128]{2,1,0:T(8,128)(2,1)} %get-tuple-element.202, s32[]{:T(128)S(6)} %copy.33, bf16[8192,128]{1,0:T(8,128)(2,1)} %get-tuple-element.211, s32[8192]{0:T(1024)S(1)} %bitcast.50, s32[512]{0:T(512)S(1)} %bitcast.53), kind=kOutput, calls=%fused_computation.7.clone.1 | convolution fusion | flops 1077936128 | bytes 2394116 | tf_op jit(solution)/shard_map/while/body/eval_jaxpr/dot_general | solution.py:77
  233.0 4.6 %fusion.43 = bf16[8,512,128]{2,1,0:T(8,128)(2,1)} fusion(bf16[8,512,128]{2,1,0:T(8,128)(2,1)} %get-tuple-element.202, s32[]{:T(128)S(6)} %copy.33, bf16[8192,128]{1,0:T(8,128)(2,1)} %get-tuple-element.211, s32[8192]{0:T(1024)S(1)} %bitcast.50, s32[512]{0:T(512)S(1)} %bitcast.53), kind=kOutput, calls=%fused_computation.7.clone.1 | convolution fusion | flops 1077936128 | bytes 2394116 | tf_op jit(solution)/shard_map/while/body/eval_jaxpr/dot_general | solution.py:77
  237.7 4.6 %fusion.43 = bf16[8,512,128]{2,1,0:T(8,128)(2,1)} fusion(bf16[8,512,128]{2,1,0:T(8,128)(2,1)} %get-tuple-element.202, s32[]{:T(128)S(6)} %copy.33, bf16[8192,128]{1,0:T(8,128)(2,1)} %get-tuple-element.211, s32[8192]{0:T(1024)S(1)} %bitcast.50, s32[512]{0:T(512)S(1)} %bitcast.53), kind=kOutput, calls=%fused_computation.7.clone.1 | convolution fusion | flops 1077936128 | bytes 2394116 | tf_op jit(solution)/shard_map/while/body/eval_jaxpr/dot_general | solution.py:77
  242.3 4.6 %fusion.43 = bf16[8,512,128]{2,1,0:T(8,128)(2,1)} fusion(bf16[8,512,128]{2,1,0:T(8,128)(2,1)} %get-tuple-element.202, s32[]{:T(128)S(6)} %copy.33, bf16[8192,128]{1,0:T(8,128)(2,1)} %get-tuple-element.211, s32[8192]{0:T(1024)S(1)} %bitcast.50, s32[512]{0:T(512)S(1)} %bitcast.53), kind=kOutput, calls=%fused_computation.7.clone.1 | convolution fusion | flops 1077936128 | bytes 2394116 | tf_op jit(solution)/shard_map/while/body/eval_jaxpr/dot_general | solution.py:77
  247.0 4.7 %fusion.43 = bf16[8,512,128]{2,1,0:T(8,128)(2,1)} fusion(bf16[8,512,128]{2,1,0:T(8,128)(2,1)} %get-tuple-element.202, s32[]{:T(128)S(6)} %copy.33, bf16[8192,128]{1,0:T(8,128)(2,1)} %get-tuple-element.211, s32[8192]{0:T(1024)S(1)} %bitcast.50, s32[512]{0:T(512)S(1)} %bitcast.53), kind=kOutput, calls=%fused_computation.7.clone.1 | convolution fusion | flops 1077936128 | bytes 2394116 | tf_op jit(solution)/shard_map/while/body/eval_jaxpr/dot_general | solution.py:77
  253.9 4.1 %fusion.17 = pred[4096]{0:T(1024)(128)(4,1)S(1)} fusion(s32[2048]{0:T(1024)S(1)} %bitcast.56), kind=kLoop, calls=%fused_computation.18 | loop fusion | flops 16773120 | bytes 12288 | tf_op jit(solution)/shard_map/reduce_or | solution.py:73
  258.0 39.7 %all-reduce.3.cloned.1.call-done = f32[1024,1024]{0,1:T(8,128)} async-done(((f32[1024,1024]{0,1:T(8,128)}), f32[1024,1024]{0,1:T(8,128)}) %all-reduce.3.cloned.1.call-update) | async-done | bytes 4194320 | tf_op jit(solution)/shard_map/psum | solution.py:66
  297.7 5.0 %broadcast_multiply_fusion = f32[1024,1024]{0,1:T(8,128)} fusion(f32[1024,1024]{0,1:T(8,128)} %all-reduce.3.cloned.1.call-done), kind=kLoop, calls=%fused_computation.33 | loop fusion | flops 1048576 | bytes 8388608 | tf_op jit(solution)/shard_map/mul | solution.py:67
  302.7 5.4 %copy.17 = f32[1024,1024]{1,0:T(8,128)} copy(f32[1024,1024]{0,1:T(8,128)} %broadcast_multiply_fusion) | data formatting | bytes 8388608
  308.0 36.2 %all-reduce.5.cloned.1.call-done = bf16[4096,128]{1,0:T(8,128)(2,1)} async-done(((bf16[4096,128]{1,0:T(8,128)(2,1)}), bf16[4096,128]{1,0:T(8,128)(2,1)}) %all-reduce.5.cloned.1.call-update) | async-done | bytes 1048592 | tf_op jit(solution)/shard_map/psum | solution.py:80
  346.8 4.5 %fusion.20 = f32[4096,128]{1,0:T(8,128)} fusion(f32[4096,128]{1,0:T(8,128)} %param.18, bf16[4096,128]{1,0:T(8,128)(2,1)} %all-reduce.5.cloned.1.call-done, f32[4096]{0:T(1024)S(1)} %get-tuple-element.114, pred[4096]{0:T(1024)(128)(4,1)S(1)} %fusion.17), kind=kLoop, calls=%fused_computation.27 | loop fusion | flops 3145728 | bytes 5263360 | tf_op jit(solution)/shard_map/jit(_where)/select_n | solution.py:82
  (113 shorter events, 102.9 us)
Async XLA Ops:
  7.2 1.7 copy-start
  8.9 2.7 copy-start.1
  8.9 2.7 copy-start.2
  8.9 2.7 copy-start.7
  13.1 1.0 copy-start.3
  120.0 94.2 %all-to-all-start = ((bf16[32,256,128]{2,1,0:T(8,128)(2,1)}), bf16[32,256,128]{2,1,0:T(8,128)(2,1)}, u32[]{:S(2)}, u32[]{:S(2)}) async-start(bf16[32,256,128]{2,1,0:T(8,128)(2,1)} %bitcast.47), calls=%async_computation | async-start | bytes 4194304 | tf_op jit(solution)/shard_map/all_to_all | solution.py:65
  128.5 169.1 %all-reduce.3.cloned.1.call-start = ((), (), s32[]{:S(2)}) async-start(), calls=%async_computation.1 | async-start | bytes 8388608 | tf_op jit(solution)/shard_map/psum | solution.py:66
  133.2 81.0 %copy-start.4 = (s32[1,32,256]{2,1,0:T(8,128)S(1)}, s32[1,32,256]{2,1,0:T(8,128)}, u32[]{:S(2)}) copy-start(s32[1,32,256]{2,1,0:T(8,128)} %param.22) | copy-start | bytes 98308
  133.2 211.1 %all-reduce.5.cloned.1.call-start = ((), (), s32[]{:S(2)}) async-start(), calls=%async_computation.2 | async-start | bytes 2097152 | tf_op jit(solution)/shard_map/psum | solution.py:80
  214.2 39.7 %copy-start.6 = (s32[1,2048]{1,0:T(1,128)S(1)}, s32[1,2048]{1,0:T(1,128)}, u32[]{:S(2)}) copy-start(s32[1,2048]{1,0:T(1,128)} %param.23) | copy-start | bytes 24580
  302.7 43.5 %copy-start.5 = (f32[4096]{0:T(1024)S(1)}, f32[4096]{0:T(1024)}, u32[]{:S(2)}) copy-start(f32[4096]{0:T(1024)} %param.19) | copy-start | bytes 49156
Sparse Core Ops, SparseCore 0:
  134.8 162.7 all-reduce.2
  300.0 44.2 all-reduce.4
where the time goes:
time: 360 us; the launch traced here: 358 us
  matrix products  97.1 us (27%)
  blocking collectives  79.4 us (22%)
  waiting for transfers between devices  76 us (21%)
  local copies, waits for them, and re-layouts  63 us (18%)
  other arithmetic  19.4 us (5%)
  between operations  14.2 us (4%)
  starting transfers between devices  8.65 us (2%)
    psum x1, blocking collectives, per_device(): weight_sum, bias_sum = lax.psum((weight_part, bias_part), ('rep', 'shard'))  79.4 us
    dot_general x16, matrix products, pick_bags(): jnp.dot(select, pooled, preferred_element_type=jnp.float32)  51.3 us
    gather x16, local copies, waits for them, and re-layouts, pick_bags(): flat_bags[positions][:, None] == bag_range[None, :]  50.3 us
    psum x1, waiting for transfers between devices, per_device(): weight_sum, bias_sum = lax.psum((weight_part, bias_part), ('rep', 'shard'))  39.7 us
    dot_general x8, matrix products, row_block(): return jnp.dot(select, incoming_rows, preferred_element_type=jnp.float32)  37.1 us
    psum x1, waiting for transfers between devices, per_device(): lax.psum(local_sums.astype(jnp.bfloat16), 'rep').astype(jnp.float32)  36.2 us
    all_to_all x1, starting transfers between devices, per_device(): lax.all_to_all(outgoing, 'shard', split_axis=0, concat_axis=0, tiled=True)  8.57 us
  transfers between devices with their start and end apart: 3, of which 2 were waited for; matrix products, arithmetic and copies ran while one was open for 17% of the time, Pallas kernels for 0%

commit v1 on v0

--- a/solution.py
+++ b/solution.py
@@ -77,7 +77,9 @@
         return jnp.dot(select, incoming_rows, preferred_element_type=jnp.float32)
 
     local_sums = blocked(shard_rows, row_block)
-    row_grads = lax.psum(local_sums.astype(jnp.bfloat16), "rep").astype(jnp.float32)
+    row_grads = jnp.sum(lax.all_gather(local_sums.astype(jnp.bfloat16), "rep"), axis=0).astype(
+        jnp.float32
+    )
     upd_table, upd_accum = adagrad_rows(emb_table, row_accum, row_grads)
     new_table = jnp.where(marks[:, None], upd_table, emb_table)
     new_accum = jnp.where(marks, upd_accum, row_accum)

time: 360 us -> 347 us (0.964)
  blocking collectives: 79.4 us -> 68 us
  waiting for transfers between devices: 76 us -> 68.7 us
    psum x1 -> x0, waiting for transfers between devices: 36.2 us -> none  [per_device(): lax.psum(local_sums.astype(jnp.bfloat16), 'rep').astype(jnp.float32)]
    all_to_all x1, waiting for transfers between devices: 0.01 us -> 25.9 us  [per_device(): lax.all_to_all(outgoing, 'shard', split_axis=0, concat_axis=0, tiled=True)]
    psum x1, blocking collectives: 79.4 us -> 68 us  [per_device(): weight_sum, bias_sum = lax.psum((weight_part, bias_part), ('rep', 'shard'))]
where the time goes in v1:
time: 347 us; the launch traced here: 345 us
  matrix products  97.3 us (28%)
  waiting for transfers between devices  68.7 us (20%)
  blocking collectives  68 us (20%)
  local copies, waits for them, and re-layouts  63 us (18%)
  other arithmetic  22.9 us (7%)
  between operations  15.6 us (4%)
  starting transfers between devices  8.66 us (2%)
    psum x1, blocking collectives, per_device(): weight_sum, bias_sum = lax.psum((weight_part, bias_part), ('rep', 'shard'))  68 us
    dot_general x16, matrix products, pick_bags(): jnp.dot(select, pooled, preferred_element_type=jnp.float32)  51.3 us
    gather x16, local copies, waits for them, and re-layouts, pick_bags(): flat_bags[positions][:, None] == bag_range[None, :]  50.3 us
    psum x1, waiting for transfers between devices, per_device(): weight_sum, bias_sum = lax.psum((weight_part, bias_part), ('rep', 'shard'))  42.8 us
    dot_general x8, matrix products, row_block(): return jnp.dot(select, incoming_rows, preferred_element_type=jnp.float32)  37.2 us
    all_to_all x1, waiting for transfers between devices, per_device(): lax.all_to_all(outgoing, 'shard', split_axis=0, concat_axis=0, tiled=True)  25.9 us
    all_to_all x1, starting transfers between devices, per_device(): lax.all_to_all(outgoing, 'shard', split_axis=0, concat_axis=0, tiled=True)  8.58 us
    unnamed x18, local copies, waits for them, and re-layouts  7.2 us
  transfers between devices with their start and end apart: 3, of which 2 were waited for; matrix products, arithmetic and copies ran while one was open for 17% of the time, Pallas kernels for 0%

profile of v1, /device:TPU:0, one launch (start us, length us, event | category | flops | bytes accessed | tf_op | source)
XLA Modules:
  0.0 344.6 jit_solution(6260563884428290327)
XLA Ops:
  18.7 102.1 %while.22 = (s32[]{:T(128)}, bf16[16,512,128]{2,1,0:T(8,128)(2,1)}, s32[16,512]{1,0:T(8,128)S(1)}, s32[8192]{0:T(1024)S(1)}, bf16[3584,128]{1,0:T(8,128)(2,1)}, /*index=5*/s32[]{:T(128)}) while((s32[]{:T(128)}, bf16[16,512,128]{2,1,0:T(8,128)(2,1)}, s32[16,512]{1,0:T(8,128)S(1)}, s32[8192]{0:T(1024)S(1)}, ...), condition=%wide.region_5.6_spmd.clone, body=%wide.region_4.5_spmd.clone.sunk | while | flops 471665152 | bytes 1067093 | solution.py:20
  41.0 3.2 fusion.45
  47.4 3.2 fusion.45
  53.8 3.2 fusion.45
  60.2 3.2 fusion.45
  120.9 8.6 %all-to-all-start = ((bf16[32,256,128]{2,1,0:T(8,128)(2,1)}), bf16[32,256,128]{2,1,0:T(8,128)(2,1)}, u32[]{:S(2)}, u32[]{:S(2)}) async-start(bf16[32,256,128]{2,1,0:T(8,128)(2,1)} %bitcast.47), calls=%async_computation | async-start | bytes 4194304 | tf_op jit(solution)/shard_map/all_to_all | solution.py:65
  129.5 4.5 %convolution_bitcast_fusion = f32[1024,1024]{0,1:T(8,128)} fusion(bf16[512,1024]{1,0:T(8,128)(2,1)S(1)} %copy-done.1, bf16[512,1024]{1,0:T(8,128)(2,1)} %param.15), kind=kOutput, calls=%fused_computation.24 | convolution fusion | flops 1075838976 | bytes 6291456 | tf_op jit(solution)/shard_map/dot_general | solution.py:43
  134.1 25.9 %all-to-all-done = bf16[32,256,128]{2,1,0:T(8,128)(2,1)} async-done(((bf16[32,256,128]{2,1,0:T(8,128)(2,1)}), bf16[32,256,128]{2,1,0:T(8,128)(2,1)}, u32[]{:S(2)}, u32[]{:S(2)}) %all-to-all-start) | async-done | bytes 2097184 | tf_op jit(solution)/shard_map/all_to_all | solution.py:65
  160.0 37.6 %while.21 = (s32[]{:T(128)}, bf16[8,512,128]{2,1,0:T(8,128)(2,1)}, s32[8,512]{1,0:T(8,128)S(1)}, s32[1,32,256]{2,1,0:T(8,128)S(1)}, bf16[8192,128]{1,0:T(8,128)(2,1)}, /*index=5*/s32[]{:T(128)}) while((s32[]{:T(128)}, bf16[8,512,128]{2,1,0:T(8,128)(2,1)}, s32[8,512]{1,0:T(8,128)S(1)}, s32[1,32,256]{2,1,0:T(8,128)S(1)}, ...), condition=%wide.region_7.8_spmd, body=%wide.region_6.7_spmd.sunk | while | flops 1077936128 | bytes 2463829 | solution.py:20
  160.0 4.7 %fusion.43 = bf16[8,512,128]{2,1,0:T(8,128)(2,1)} fusion(bf16[8,512,128]{2,1,0:T(8,128)(2,1)} %get-tuple-element.207, s32[]{:T(128)S(6)} %copy.34, bf16[8192,128]{1,0:T(8,128)(2,1)} %get-tuple-element.216, s32[8192]{0:T(1024)S(1)} %bitcast.50, s32[512]{0:T(512)S(1)} %bitcast.53), kind=kOutput, calls=%fused_computation.7.clone.1 | convolution fusion | flops 1077936128 | bytes 2394116 | tf_op jit(solution)/shard_map/while/body/eval_jaxpr/dot_general | solution.py:77
  164.8 4.7 %fusion.43 = bf16[8,512,128]{2,1,0:T(8,128)(2,1)} fusion(bf16[8,512,128]{2,1,0:T(8,128)(2,1)} %get-tuple-element.207, s32[]{:T(128)S(6)} %copy.34, bf16[8192,128]{1,0:T(8,128)(2,1)} %get-tuple-element.216, s32[8192]{0:T(1024)S(1)} %bitcast.50, s32[512]{0:T(512)S(1)} %bitcast.53), kind=kOutput, calls=%fused_computation.7.clone.1 | convolution fusion | flops 1077936128 | bytes 2394116 | tf_op jit(solution)/shard_map/while/body/eval_jaxpr/dot_general | solution.py:77
  169.5 4.6 %fusion.43 = bf16[8,512,128]{2,1,0:T(8,128)(2,1)} fusion(bf16[8,512,128]{2,1,0:T(8,128)(2,1)} %get-tuple-element.207, s32[]{:T(128)S(6)} %copy.34, bf16[8192,128]{1,0:T(8,128)(2,1)} %get-tuple-element.216, s32[8192]{0:T(1024)S(1)} %bitcast.50, s32[512]{0:T(512)S(1)} %bitcast.53), kind=kOutput, calls=%fused_computation.7.clone.1 | convolution fusion | flops 1077936128 | bytes 2394116 | tf_op jit(solution)/shard_map/while/body/eval_jaxpr/dot_general | solution.py:77
  174.2 4.7 %fusion.43 = bf16[8,512,128]{2,1,0:T(8,128)(2,1)} fusion(bf16[8,512,128]{2,1,0:T(8,128)(2,1)} %get-tuple-element.207, s32[]{:T(128)S(6)} %copy.34, bf16[8192,128]{1,0:T(8,128)(2,1)} %get-tuple-element.216, s32[8192]{0:T(1024)S(1)} %bitcast.50, s32[512]{0:T(512)S(1)} %bitcast.53), kind=kOutput, calls=%fused_computation.7.clone.1 | convolution fusion | flops 1077936128 | bytes 2394116 | tf_op jit(solution)/shard_map/while/body/eval_jaxpr/dot_general | solution.py:77
  178.9 4.6 %fusion.43 = bf16[8,512,128]{2,1,0:T(8,128)(2,1)} fusion(bf16[8,512,128]{2,1,0:T(8,128)(2,1)} %get-tuple-element.207, s32[]{:T(128)S(6)} %copy.34, bf16[8192,128]{1,0:T(8,128)(2,1)} %get-tuple-element.216, s32[8192]{0:T(1024)S(1)} %bitcast.50, s32[512]{0:T(512)S(1)} %bitcast.53), kind=kOutput, calls=%fused_computation.7.clone.1 | convolution fusion | flops 1077936128 | bytes 2394116 | tf_op jit(solution)/shard_map/while/body/eval_jaxpr/dot_general | solution.py:77
  183.6 4.6 %fusion.43 = bf16[8,512,128]{2,1,0:T(8,128)(2,1)} fusion(bf16[8,512,128]{2,1,0:T(8,128)(2,1)} %get-tuple-element.207, s32[]{:T(128)S(6)} %copy.34, bf16[8192,128]{1,0:T(8,128)(2,1)} %get-tuple-element.216, s32[8192]{0:T(1024)S(1)} %bitcast.50, s32[512]{0:T(512)S(1)} %bitcast.53), kind=kOutput, calls=%fused_computation.7.clone.1 | convolution fusion | flops 1077936128 | bytes 2394116 | tf_op jit(solution)/shard_map/while/body/eval_jaxpr/dot_general | solution.py:77
  188.3 4.6 %fusion.43 = bf16[8,512,128]{2,1,0:T(8,128)(2,1)} fusion(bf16[8,512,128]{2,1,0:T(8,128)(2,1)} %get-tuple-element.207, s32[]{:T(128)S(6)} %copy.34, bf16[8192,128]{1,0:T(8,128)(2,1)} %get-tuple-element.216, s32[8192]{0:T(1024)S(1)} %bitcast.50, s32[512]{0:T(512)S(1)} %bitcast.53), kind=kOutput, calls=%fused_computation.7.clone.1 | convolution fusion | flops 1077936128 | bytes 2394116 | tf_op jit(solution)/shard_map/while/body/eval_jaxpr/dot_general | solution.py:77
  192.9 4.6 %fusion.43 = bf16[8,512,128]{2,1,0:T(8,128)(2,1)} fusion(bf16[8,512,128]{2,1,0:T(8,128)(2,1)} %get-tuple-element.207, s32[]{:T(128)S(6)} %copy.34, bf16[8192,128]{1,0:T(8,128)(2,1)} %get-tuple-element.216, s32[8192]{0:T(1024)S(1)} %bitcast.50, s32[512]{0:T(512)S(1)} %bitcast.53), kind=kOutput, calls=%fused_computation.7.clone.1 | convolution fusion | flops 1077936128 | bytes 2394116 | tf_op jit(solution)/shard_map/while/body/eval_jaxpr/dot_general | solution.py:77
  200.7 68.0 %psum.15 = f32[1024]{0:T(1024)S(1)} all-reduce(f32[1024]{0:T(1024)S(1)} %convert_reduce_fusion), channel_id=1, replica_groups=mesh['rep'=4,'shard'=32] {'rep','shard'}, use_global_device_ids=true, to_apply=%region_2.3 | all-reduce | flops 1024 | bytes 8192 | tf_op jit(solution)/shard_map/psum | solution.py:66
  269.3 4.1 %fusion.17 = pred[4096]{0:T(1024)(128)(4,1)S(1)} fusion(s32[2048]{0:T(1024)S(1)} %bitcast.56), kind=kLoop, calls=%fused_computation.18 | loop fusion | flops 16773120 | bytes 12288 | tf_op jit(solution)/shard_map/reduce_or | solution.py:73
  273.5 42.8 %all-reduce.2.cloned.1.call-done = f32[1024,1024]{0,1:T(8,128)} async-done(((f32[1024,1024]{0,1:T(8,128)}), f32[1024,1024]{0,1:T(8,128)}) %all-reduce.2.cloned.1.call-update) | async-done | bytes 4194320 | tf_op jit(solution)/shard_map/psum | solution.py:66
  316.3 5.0 %broadcast_multiply_fusion = f32[1024,1024]{0,1:T(8,128)} fusion(f32[1024,1024]{0,1:T(8,128)} %all-reduce.2.cloned.1.call-done), kind=kLoop, calls=%fused_computation.33 | loop fusion | flops 1048576 | bytes 8388608 | tf_op jit(solution)/shard_map/mul | solution.py:67
  321.3 5.3 %copy.18 = f32[1024,1024]{1,0:T(8,128)} copy(f32[1024,1024]{0,1:T(8,128)} %broadcast_multiply_fusion) | data formatting | bytes 8388608
  326.6 3.5 %reduce_sum.31 = bf16[4096,128]{1,0:T(8,128)(2,1)S(1)} reduce(bf16[4,4096,128]{2,1,0:T(8,128)(2,1)} %all-gather.2.cloned.1.call-done, bf16[]{:T(256)} %constant.42.clone.1), dimensions={0}, to_apply=%region_8.9 | reduce | flops 1572864 | bytes 5242882 | tf_op jit(solution)/shard_map/reduce_sum | solution.py:80
  331.4 5.8 %fusion.20 = f32[4096,128]{1,0:T(8,128)} fusion(f32[4096,128]{1,0:T(8,128)} %param.18, bf16[4096,128]{1,0:T(8,128)(2,1)S(1)} %reduce_sum.31, f32[4096]{0:T(1024)S(1)} %get-tuple-element.119, pred[4096]{0:T(1024)(128)(4,1)S(1)} %fusion.17), kind=kLoop, calls=%fused_computation.27 | loop fusion | flops 3145728 | bytes 5263360 | tf_op jit(solution)/shard_map/jit(_where)/select_n | solution.py:84
  (114 shorter events, 105.0 us)
Async XLA Ops:
  8.0 1.7 copy-start
  9.7 2.7 copy-start.1
  9.7 2.7 copy-start.2
  9.7 2.7 copy-start.7
  13.9 1.0 copy-start.3
  120.9 39.1 %all-to-all-start = ((bf16[32,256,128]{2,1,0:T(8,128)(2,1)}), bf16[32,256,128]{2,1,0:T(8,128)(2,1)}, u32[]{:S(2)}, u32[]{:S(2)}) async-start(bf16[32,256,128]{2,1,0:T(8,128)(2,1)} %bitcast.47), calls=%async_computation | async-start | bytes 4194304 | tf_op jit(solution)/shard_map/all_to_all | solution.py:65
  129.4 186.9 %all-reduce.2.cloned.1.call-start = ((), (), s32[]{:S(2)}) async-start(), calls=%async_computation.1 | async-start | bytes 8388608 | tf_op jit(solution)/shard_map/psum | solution.py:66
  134.0 26.0 %copy-start.4 = (s32[1,32,256]{2,1,0:T(8,128)S(1)}, s32[1,32,256]{2,1,0:T(8,128)}, u32[]{:S(2)}) copy-start(s32[1,32,256]{2,1,0:T(8,128)} %param.22) | copy-start | bytes 98308
  134.1 192.6 %all-gather.2.cloned.1.call-start = ((), (), s32[]{:S(2)}) async-start(), calls=%async_computation.2 | async-start | bytes 5242880 | tf_op jit(solution)/shard_map/all_gather | solution.py:80
  197.6 71.8 %copy-start.6 = (s32[1,2048]{1,0:T(1,128)S(1)}, s32[1,2048]{1,0:T(1,128)}, u32[]{:S(2)}) copy-start(s32[1,2048]{1,0:T(1,128)} %param.23) | copy-start | bytes 24580
  326.6 4.1 %copy-start.5 = (f32[4096]{0:T(1024)S(1)}, f32[4096]{0:T(1024)}, u32[]{:S(2)}) copy-start(f32[4096]{0:T(1024)} %param.19) | copy-start | bytes 49156
Sparse Core Ops, SparseCore 0:
  135.8 180.4 all-reduce.1
Sparse Core Ops, SparseCore 1:
  197.7 48.4 all-gather.1
